TPU v7x, 32 devices: a whole 2x2x4 slice. The times are simulated.
32 devices in a mesh: blk: 16 (over z, y, core), rel: 2 (over x).
Axes of the slice: x: 2, y: 2, z: 4, core: 2. Of those that a mesh axis runs over, the one named last changes fastest.
Arguments:
- words: bfloat16 [4096, 800], P('blk'), may hold values from -1.5 to 1.5
- contexts: bfloat16 [4096, 800], P('blk'), may hold values from -1.5 to 1.5
- relations: bfloat16 [1024, 800], P(('blk', 'rel')), may hold values from -6 to 6
- word_index: int32 [8192], P(('blk', 'rel')), may hold values from 0 to 255
- context_index: int32 [8192], P(('blk', 'rel')), may hold values from 0 to 255
- rel_slot: int32 [8192], P(('blk', 'rel')), may hold values from 0 to 63, as said below
- neg_index: int32 [32, 1024], P(('blk', 'rel')), may hold values from 0 to 255
- requests: int32 [16, 2, 16, 2, 2], P('blk', 'rel'), may hold values from 0 to 31, as said below
- counts: int32 [16, 2, 16, 2], P('blk', 'rel'), may hold values from 0 to 2, as said below
Outputs:
- word_grad: bfloat16 [4096, 800], P('blk')
- context_grad: bfloat16 [4096, 800], P('blk')
- relation_grad: float32 [1024, 800], P(('blk', 'rel'))
Inputs may be any that keep to these rules, and one draw needn't show every extreme that they name: counts[b, r, b2, r2] is how many entries of the list of device (b, r) to owner (b2, r2) are live; each device's list to itself is full, and so are all lists to one owner. requests[b, r, b2, r2, k] is a row among the 32 relation rows of owner (b2, r2); the live entries of one list are distinct and come first, the others are 0. rel_slot of a triple of device (b, r) is a live slot s = (b2 * 2 + r2) * 2 + k of that device, with k < counts[b, r, b2, r2].
All inputs are finite; a program needn't handle non-finite values.
Results may differ from a plain program's by a relative error of at most 0.013.
Values may be sent and summed in bfloat16 or wider, within the bound.
No kernel may reach another device: no remote copies, remote signals or barrier semaphores. Data moves between devices by JAX's collectives and lax.ppermute only.
A program may use at most 64 MiB of HBM per device.

v0:
```python
import jax
import jax.numpy as jnp
from jax import lax
from jax.sharding import PartitionSpec as P


def passed_along(shard, axis, by):
    length = lax.axis_size(axis)
    return lax.ppermute(shard, axis, [(i, (i + by) % length) for i in range(length)])


def complex_product(left_vec, right_vec, half_width):
    left_re, left_im = (left_vec[:, :half_width], left_vec[:, half_width:])
    right_re, right_im = (right_vec[:, :half_width], right_vec[:, half_width:])
    return jnp.concatenate(
        [left_re * right_re - left_im * right_im, left_re * right_im + left_im * right_re], axis=1
    )


def conj_product(grad_vec, other_vec, half_width):
    grad_re, grad_im = (grad_vec[:, :half_width], grad_vec[:, half_width:])
    other_re, other_im = (other_vec[:, :half_width], other_vec[:, half_width:])
    return jnp.concatenate(
        [grad_re * other_re + grad_im * other_im, grad_im * other_re - grad_re * other_im], axis=1
    )


def one_hot_rows(index_ids, row_total):
    return (jnp.arange(row_total)[:, None] == index_ids[None, :]).astype(jnp.bfloat16)


def spread_rows(selector, terms):
    upper = terms.astype(jnp.bfloat16)
    lower = (terms - upper.astype(jnp.float32)).astype(jnp.bfloat16)
    return jnp.dot(selector, upper, preferred_element_type=jnp.float32) + jnp.dot(
        selector, lower, preferred_element_type=jnp.float32
    )


def shards(
    words, contexts, relations, word_index, context_index, rel_slot, neg_index, requests, counts
):
    row_width = words.shape[1]
    half_width = row_width // 2
    part_count = lax.axis_size("blk")
    split_count = lax.axis_size("rel")
    slot_count = requests.shape[-1]
    owned_rows = relations.shape[0]
    block_count = neg_index.shape[0]
    block_size = word_index.shape[0] // block_count
    part_rows = contexts.shape[0]
    neg_scale = float(neg_index.shape[1]) ** (-0.5)
    held_rows = passed_along(contexts, "blk", 1)
    wanted = requests[0, 0]
    incoming = lax.all_to_all(
        lax.all_to_all(wanted, "blk", split_axis=0, concat_axis=0, tiled=True),
        "rel",
        split_axis=1,
        concat_axis=1,
        tiled=True,
    )
    picked = relations[incoming.reshape(-1)].reshape(part_count, split_count, slot_count, row_width)
    fetched = lax.all_to_all(
        lax.all_to_all(picked, "blk", split_axis=0, concat_axis=0, tiled=True),
        "rel",
        split_axis=1,
        concat_axis=1,
        tiled=True,
    )
    slot_table = fetched.reshape(-1, row_width)
    slot_total = slot_table.shape[0]
    live_mask = (
        (jnp.arange(slot_count)[None, None, :] < counts[0, 0][:, :, None])
        .reshape(-1)
        .astype(jnp.float32)
    )
    word_used = words[word_index]
    ctx_used = held_rows[context_index]
    rel_used = slot_table[rel_slot]
    query = complex_product(
        word_used.astype(jnp.float32), rel_used.astype(jnp.float32), half_width
    ).astype(jnp.bfloat16)
    positive = jnp.einsum("td,td->t", query, ctx_used, preferred_element_type=jnp.float32)
    pos_grad = -jax.nn.sigmoid(-positive)
    ctx_start = spread_rows(
        one_hot_rows(context_index, part_rows), pos_grad[:, None] * query.astype(jnp.float32)
    )

    def block_step(ctx_total, inputs_one):
        query_block, ctx_block, neg_block, pos_block = inputs_one
        selector = one_hot_rows(neg_block, part_rows)
        neg_rows = lax.dot_general(
            selector, held_rows, (((0,), (0,)), ((), ())), preferred_element_type=jnp.float32
        ).astype(jnp.bfloat16)
        scores = lax.dot_general(
            query_block, neg_rows, (((1,), (1,)), ((), ())), preferred_element_type=jnp.float32
        )
        neg_grad = (jax.nn.sigmoid(scores) * neg_scale).astype(jnp.bfloat16)
        query_grad = pos_block[:, None] * ctx_block.astype(jnp.float32) + jnp.dot(
            neg_grad, neg_rows, preferred_element_type=jnp.float32
        )
        back_rows = lax.dot_general(
            neg_grad, query_block, (((0,), (0,)), ((), ())), preferred_element_type=jnp.float32
        )
        return (ctx_total + spread_rows(selector, back_rows), query_grad)

    ctx_part, query_grads = lax.scan(
        block_step,
        ctx_start,
        (
            query.reshape(block_count, block_size, row_width),
            ctx_used.reshape(block_count, block_size, row_width),
            neg_index,
            pos_grad.reshape(block_count, block_size),
        ),
    )
    query_grads = query_grads.reshape(-1, row_width)
    word_part = spread_rows(
        one_hot_rows(word_index, words.shape[0]),
        conj_product(query_grads, rel_used.astype(jnp.float32), half_width),
    )
    slot_grad = spread_rows(
        one_hot_rows(rel_slot, slot_total),
        conj_product(query_grads, word_used.astype(jnp.float32), half_width),
    )
    slot_grad = slot_grad + 0.02 * live_mask[:, None] * slot_table.astype(jnp.float32)
    word_sum, ctx_sum = (
        lax.psum(word_part.astype(jnp.bfloat16), "rel").astype(jnp.float32),
        lax.psum(ctx_part.astype(jnp.bfloat16), "rel").astype(jnp.float32),
    )
    outgoing = slot_grad.reshape(part_count, split_count, slot_count, row_width)
    returned = lax.all_to_all(
        lax.all_to_all(
            outgoing.astype(jnp.bfloat16), "blk", split_axis=0, concat_axis=0, tiled=True
        ),
        "rel",
        split_axis=1,
        concat_axis=1,
        tiled=True,
    ).astype(outgoing.dtype)
    owner_map = (incoming.reshape(-1)[None, :] == jnp.arange(owned_rows)[:, None]).astype(
        jnp.float32
    )
    relation_grad = jnp.dot(
        owner_map,
        returned.reshape(-1, row_width),
        precision=lax.Precision.HIGHEST,
        preferred_element_type=jnp.float32,
    )
    return (word_sum.astype(jnp.bfloat16), ctx_sum.astype(jnp.bfloat16), relation_grad)


def solution(mesh):
    return jax.shard_map(
        shards,
        mesh=mesh,
        in_specs=(
            P("blk", None),
            P("blk", None),
            P(("blk", "rel"), None),
            P(("blk", "rel")),
            P(("blk", "rel")),
            P(("blk", "rel")),
            P(("blk", "rel"), None),
            P("blk", "rel", None, None, None),
            P("blk", "rel", None, None),
        ),
        out_specs=(P("blk", None), P("blk", None), P(("blk", "rel"), None)),
        check_vma=False,
    )
```

profile of v0, /device:TPU:0, one launch (start us, length us, event | category | flops | bytes accessed | tf_op | source)
XLA Modules:
  0.0 111.6 jit_solution(12965899353701402154)
XLA Ops:
  7.2 1.4 %copy.51 = s32[16,2,2]{2,1,0:T(2,128)} copy(s32[16,2,2]{0,2,1:T(2,128)} %bitcast.14) | data formatting | bytes 512 | tf_op jit(solution)/shard_map/squeeze | solution.py:54
  8.6 7.4 %all-to-all-start = ((s32[16,2,2]{2,1,0:T(2,128)}), s32[16,2,2]{2,1,0:T(2,128)S(1)}, u32[]{:S(2)}, u32[]{:S(2)}) async-start(s32[16,2,2]{2,1,0:T(2,128)} %copy.51), calls=%async_computation | async-start | bytes 32768 | tf_op jit(solution)/shard_map/all_to_all | solution.py:56
  16.0 2.0 %copy.57 = bf16[256,800]{1,0:T(8,128)(2,1)} copy(bf16[256,800]{0,1:T(8,128)(2,1)} %param.10) | data formatting | bytes 819200 | tf_op args[1]
  18.0 0.4 collective-permute-start
  18.4 0.7 compare_select_fusion.2
  19.1 0.7 compare_select_fusion.3
  19.8 0.8 copy.60
  20.5 0.1 compare_select_fusion
  20.6 1.9 %all-to-all-done = s32[16,2,2]{2,1,0:T(2,128)S(1)} async-done(((s32[16,2,2]{2,1,0:T(2,128)}), s32[16,2,2]{2,1,0:T(2,128)S(1)}, u32[]{:S(2)}, u32[]{:S(2)}) %all-to-all-start) | async-done | bytes 288 | tf_op jit(solution)/shard_map/all_to_all | solution.py:56
  22.5 0.7 copy.52
  23.2 3.2 %all-to-all-start.1 = ((s32[16,2,2]{0,2,1:T(2,128)}), s32[16,2,2]{0,2,1:T(2,128)S(1)}, u32[]{:S(2)}, u32[]{:S(2)}) async-start(s32[16,2,2]{0,2,1:T(2,128)} %copy.52), calls=%async_computation.1 | async-start | bytes 4096 | tf_op jit(solution)/shard_map/all_to_all | solution.py:55
  26.4 3.7 %all-to-all-done.1 = s32[16,2,2]{0,2,1:T(2,128)S(1)} async-done(((s32[16,2,2]{0,2,1:T(2,128)}), s32[16,2,2]{0,2,1:T(2,128)S(1)}, u32[]{:S(2)}, u32[]{:S(2)}) %all-to-all-start.1) | async-done | bytes 288 | tf_op jit(solution)/shard_map/all_to_all | solution.py:55
  30.2 0.1 copy.53
  30.3 0.1 reshape.85
  30.4 0.7 gather_fusion.1
  31.1 0.7 reshape.86
  31.8 3.9 %all-to-all-start.2 = ((bf16[16,2,2,800]{3,2,1,0:T(2,128)(2,1)}), bf16[16,2,2,800]{3,2,1,0:T(2,128)(2,1)S(1)}, u32[]{:S(2)}, u32[]{:S(2)}) async-start(bf16[16,2,2,800]{3,2,1,0:T(2,128)(2,1)} %reshape.86), calls=%async_computation.2 | async-start | bytes 229376 | tf_op jit(solution)/shard_map/all_to_all | solution.py:64
  35.7 7.7 %all-to-all-done.2 = bf16[16,2,2,800]{3,2,1,0:T(2,128)(2,1)S(1)} async-done(((bf16[16,2,2,800]{3,2,1,0:T(2,128)(2,1)}), bf16[16,2,2,800]{3,2,1,0:T(2,128)(2,1)S(1)}, u32[]{:S(2)}, u32[]{:S(2)}) %all-to-all-start.2) | async-done | bytes 102432 | tf_op jit(solution)/shard_map/all_to_all | solution.py:64
  43.4 0.7 copy.54
  44.1 3.4 %all-to-all-start.3 = ((bf16[16,2,2,800]{3,2,0,1:T(2,128)(2,1)}), bf16[16,2,2,800]{3,2,0,1:T(2,128)(2,1)S(1)}, u32[]{:S(2)}, u32[]{:S(2)}) async-start(bf16[16,2,2,800]{3,2,0,1:T(2,128)(2,1)} %copy.54), calls=%async_computation.3 | async-start | bytes 229376 | tf_op jit(solution)/shard_map/all_to_all | solution.py:63
  47.5 0.0 all-reduce.3.cloned.1.call-start
  47.5 0.2 copy.49
  47.8 1.2 %gather_fusion = bf16[256,800]{1,0:T(8,128)(2,1)S(1)} fusion(bf16[256,800]{1,0:T(8,128)(2,1)S(1)} %copy.49, s32[1024]{0:T(1024)S(1)} %pad_clamp_fusion.3), kind=kCustom, calls=%fused_computation | custom fusion | bytes 820224 | tf_op jit(solution)/shard_map/gather | solution.py:77
  49.0 0.2 copy.50
  49.2 0.1 convert_element_type.91
  49.3 0.1 mul.94
  49.4 2.5 %all-to-all-done.3 = bf16[16,2,2,800]{3,2,0,1:T(2,128)(2,1)S(1)} async-done(((bf16[16,2,2,800]{3,2,0,1:T(2,128)(2,1)}), bf16[16,2,2,800]{3,2,0,1:T(2,128)(2,1)S(1)}, u32[]{:S(2)}, u32[]{:S(2)}) %all-to-all-start.3) | async-done | bytes 102432 | tf_op jit(solution)/shard_map/all_to_all | solution.py:63
  51.8 0.1 copy.55
  51.9 0.1 reshape.87
  52.0 1.2 %gather_fusion.2 = bf16[256,800]{1,0:T(8,128)(2,1)S(1)} fusion(bf16[64,800]{1,0:T(8,128)(2,1)S(1)} %reshape.87, s32[1024]{0:T(1024)S(1)} %pad_clamp_fusion.1), kind=kCustom, calls=%fused_computation.2 | custom fusion | bytes 820224 | tf_op jit(solution)/shard_map/gather | solution.py:79
  53.2 0.2 copy.56
  53.4 0.1 convert_element_type.92
  53.5 0.1 subtract_convert_fusion.8
  53.6 0.1 fusion.41
  53.7 1.2 %copy.66 = f32[256,800]{1,0:T(8,128)} copy(f32[256,800]{0,1:T(8,128)S(1)} %fusion.41) | data formatting | bytes 1638400
  54.9 0.7 convolution_convert_fusion
  55.6 0.9 fusion.6
  56.5 1.5 %fusion.42 = f32[256,800]{0,1:T(8,128)} fusion(bf16[256,1024]{1,0:T(8,128)(2,1)S(1)} %fusion.6, bf16[1024,800]{0,1:T(8,128)(2,1)S(1)} %convolution_convert_fusion), kind=kOutput, calls=%fused_computation.81 | convolution fusion | flops 419430400 | bytes 2981888 | tf_op jit(solution)/shard_map/while/body/eval_jaxpr/dot_general | solution.py:99
  58.0 2.3 %fusion.40 = f32[1024,800]{0,1:T(8,128)} fusion(bf16[256,1024]{1,0:T(8,128)(2,1)S(1)} %fusion.6, bf16[256,400]{0,1:T(8,128)(2,1)S(1)} %get-tuple-element.34, bf16[256,400]{0,1:T(8,128)(2,1)S(1)} %get-tuple-element.33), kind=kOutput, calls=%fused_computation.79 | convolution fusion | flops 420249600 | bytes 4210688 | tf_op jit(solution)/shard_map/while/body/eval_jaxpr/dot_general | solution.py:102
  60.3 1.2 %gather_fusion.3 = bf16[256,800]{1,0:T(8,128)(2,1)S(1)} fusion(bf16[256,800]{1,0:T(8,128)(2,1)S(1)} %collective-permute-done, s32[1024]{0:T(1024)S(1)} %pad_clamp_fusion), kind=kCustom, calls=%fused_computation.3 | custom fusion | bytes 820224 | tf_op jit(solution)/shard_map/gather | solution.py:78
  61.5 0.2 copy.58
  61.7 1.4 %multiply_reduce_fusion = f32[256]{0:T(256)S(1)} fusion(f32[256,800]{1,0:T(8,128)} %copy.66, bf16[256,800]{1,0:T(8,128)(2,1)S(1)} %gather_fusion.3), kind=kLoop, calls=%fused_computation.23 | loop fusion | flops 614144 | bytes 1229824 | tf_op jit(solution)/shard_map/td,td->t/dot_general | solution.py:83
  63.1 0.3 fusion.15
  63.5 0.1 multiply_add_fusion
  63.6 1.0 multiply_add_fusion.1
  64.6 0.3 convolution_add_fusion.1
  64.9 0.8 copy-done.1
  65.7 0.6 fusion
  66.3 0.3 fusion.19
  66.6 1.1 fusion.7
  67.7 1.4 %fusion.8 = bf16[256,800]{0,1:T(8,128)(2,1)} fusion(f32[256,800]{0,1:T(8,128)S(1)} %convolution_add_fusion.1, f32[256,800]{0,1:T(8,128)S(1)} %fusion, f32[1024,800]{0,1:T(8,128)S(1)} %copy-done.1, s32[1024]{0:T(1024)S(1)} %bitcast.13), kind=kOutput, calls=%fused_computation.18 | convolution fusion | flops 421126144 | bytes 5328896 | tf_op jit(solution)/shard_map/while/body/eval_jaxpr/dot_general | solution.py:35
  69.2 0.3 fusion.21
  69.5 0.3 fusion.10
  69.8 10.3 %all_to_all.30 = bf16[16,2,2,800]{3,2,1,0:T(2,128)(2,1)S(1)} all-to-all(bf16[16,2,2,800]{3,2,1,0:T(2,128)(2,1)S(1)} %convert_element_type.113), channel_id=1, replica_groups=mesh['blk'=16,'rel'=2] {'blk'}, dimensions={0} | all-to-all | bytes 204800 | tf_op jit(solution)/shard_map/all_to_all | solution.py:133
  80.1 0.7 copy.61
  80.8 3.4 %all-to-all-start.5 = ((bf16[16,2,2,800]{3,2,0,1:T(2,128)(2,1)}), bf16[16,2,2,800]{3,2,0,1:T(2,128)(2,1)S(1)}, u32[]{:S(2)}, u32[]{:S(2)}) async-start(bf16[16,2,2,800]{3,2,0,1:T(2,128)(2,1)} %copy.61), calls=%async_computation.5 | async-start | bytes 229376 | tf_op jit(solution)/shard_map/all_to_all | solution.py:132
  84.2 0.1 eq.86
  84.3 4.3 %all-to-all-done.5 = bf16[16,2,2,800]{3,2,0,1:T(2,128)(2,1)S(1)} async-done(((bf16[16,2,2,800]{3,2,0,1:T(2,128)(2,1)}), bf16[16,2,2,800]{3,2,0,1:T(2,128)(2,1)S(1)}, u32[]{:S(2)}, u32[]{:S(2)}) %all-to-all-start.5) | async-done | bytes 102432 | tf_op jit(solution)/shard_map/all_to_all | solution.py:132
  88.5 0.1 copy.62
  88.6 0.1 reshape.88
  88.7 0.8 fusion.33
  89.5 11.7 %all-reduce.3.cloned.1.call-done = (bf16[256,800]{0,1:T(8,128)(2,1)}, bf16[256,800]{0,1:T(8,128)(2,1)}) async-done(((bf16[256,800]{0,1:T(8,128)(2,1)}, bf16[256,800]{0,1:T(8,128)(2,1)}), (bf16[256,800]{0,1:T(8,128)(2,1)}, bf16[256,800]{0,1:T(8,128)(2,1)})) %all-reduce.3.cloned.1.call-update) | async-done | bytes 819216 | tf_op jit(solution)/shard_map/psum | solution.py:128
  101.2 1.8 %copy.69 = bf16[256,800]{0,1:T(8,128)(2,1)} copy(bf16[256,800]{0,1:T(8,128)(2,1)} %get-tuple-element.37) | data formatting | bytes 819200
  103.0 1.8 %copy.70 = bf16[256,800]{0,1:T(8,128)(2,1)} copy(bf16[256,800]{0,1:T(8,128)(2,1)} %get-tuple-element.38) | data formatting | bytes 819200
  (27 shorter events, 0.2 us)
Async XLA Ops:
  7.2 23.2 %copy-start = (bf16[32,800]{1,0:T(8,128)(2,1)S(1)}, bf16[32,800]{1,0:T(8,128)(2,1)}, u32[]{:S(2)}) copy-start(bf16[32,800]{1,0:T(8,128)(2,1)} %param.11) | copy-start | bytes 153604
  7.2 28.5 %copy-start.7 = (s32[256]{0:T(256)S(1)}, s32[256]{0:T(256)}, u32[]{:S(2)}) copy-start(s32[256]{0:T(256)} %param.13) | copy-start | bytes 3076
  7.2 40.3 %copy-start.4 = (bf16[256,800]{0,1:T(8,128)(2,1)S(1)}, bf16[256,800]{0,1:T(8,128)(2,1)}, u32[]{:S(2)}) copy-start(bf16[256,800]{0,1:T(8,128)(2,1)} %param.9) | copy-start | bytes 1228804
  8.6 13.9 %all-to-all-start = ((s32[16,2,2]{2,1,0:T(2,128)}), s32[16,2,2]{2,1,0:T(2,128)S(1)}, u32[]{:S(2)}, u32[]{:S(2)}) async-start(s32[16,2,2]{2,1,0:T(2,128)} %copy.51), calls=%async_computation | async-start | bytes 32768 | tf_op jit(solution)/shard_map/all_to_all | solution.py:56
  18.0 36.9 %collective-permute-start = (bf16[256,800]{1,0:T(8,128)(2,1)}, bf16[256,800]{1,0:T(8,128)(2,1)S(1)}, u32[]{:S(2)}, u32[]{:S(2)}) collective-permute-start(bf16[256,800]{1,0:T(8,128)(2,1)} %copy.57), channel_id=1, source_target_pairs={{0,2},{2,4},{4,6},{6,8},{8,10},{10,12},{12,14},{14,16},{16,18},{18... | collective-permute-start | bytes 1228808 | tf_op jit(solution)/shard_map/ppermute | solution.py:9
  23.2 7.0 %all-to-all-start.1 = ((s32[16,2,2]{0,2,1:T(2,128)}), s32[16,2,2]{0,2,1:T(2,128)S(1)}, u32[]{:S(2)}, u32[]{:S(2)}) async-start(s32[16,2,2]{0,2,1:T(2,128)} %copy.52), calls=%async_computation.1 | async-start | bytes 4096 | tf_op jit(solution)/shard_map/all_to_all | solution.py:55
  31.8 11.6 %all-to-all-start.2 = ((bf16[16,2,2,800]{3,2,1,0:T(2,128)(2,1)}), bf16[16,2,2,800]{3,2,1,0:T(2,128)(2,1)S(1)}, u32[]{:S(2)}, u32[]{:S(2)}) async-start(bf16[16,2,2,800]{3,2,1,0:T(2,128)(2,1)} %reshape.86), calls=%async_computation.2 | async-start | bytes 229376 | tf_op jit(solution)/shard_map/all_to_all | solution.py:64
  44.1 7.7 %all-to-all-start.3 = ((bf16[16,2,2,800]{3,2,0,1:T(2,128)(2,1)}), bf16[16,2,2,800]{3,2,0,1:T(2,128)(2,1)S(1)}, u32[]{:S(2)}, u32[]{:S(2)}) async-start(bf16[16,2,2,800]{3,2,0,1:T(2,128)(2,1)} %copy.54), calls=%async_computation.3 | async-start | bytes 229376 | tf_op jit(solution)/shard_map/all_to_all | solution.py:63
  47.5 53.8 %all-reduce.3.cloned.1.call-start = ((), (), s32[]{:S(2)}) async-start(), calls=%async_computation.6 | async-start | bytes 1638400 | tf_op jit(solution)/shard_map/psum | solution.py:128
  53.6 1.3 %copy-start.5 = (s32[1,1024]{1,0:T(1,128)S(1)}, s32[1,1024]{1,0:T(1,128)}, u32[]{:S(2)}) copy-start(s32[1,1024]{1,0:T(1,128)} %param.15) | copy-start | bytes 12292
  61.7 1.8 %copy-start.3 = (f32[256,800]{0,1:T(8,128)S(1)}, f32[256,800]{0,1:T(8,128)}, u32[]{:S(2)}) copy-start(f32[256,800]{0,1:T(8,128)} %fusion.42) | copy-start | bytes 2457604
  63.6 2.1 %copy-start.1 = (f32[1024,800]{0,1:T(8,128)S(1)}, f32[1024,800]{0,1:T(8,128)}, u32[]{:S(2)}) copy-start(f32[1024,800]{0,1:T(8,128)} %fusion.40) | copy-start | bytes 9830404
  65.7 0.7 copy-start.6
  67.7 1.5 %copy-start.2 = (f32[256,400]{0,1:T(8,128)S(1)}, f32[256,400]{0,1:T(8,128)}, u32[]{:S(2)}) copy-start(f32[256,400]{0,1:T(8,128)} %get-tuple-element.22) | copy-start | bytes 1228804
  67.7 1.5 %copy-start.8 = (s32[256]{0:T(256)S(1)}, s32[256]{0:T(256)}, u32[]{:S(2)}) copy-start(s32[256]{0:T(256)} %param.14) | copy-start | bytes 3076
  80.8 7.7 %all-to-all-start.5 = ((bf16[16,2,2,800]{3,2,0,1:T(2,128)(2,1)}), bf16[16,2,2,800]{3,2,0,1:T(2,128)(2,1)S(1)}, u32[]{:S(2)}, u32[]{:S(2)}) async-start(bf16[16,2,2,800]{3,2,0,1:T(2,128)(2,1)} %copy.61), calls=%async_computation.5 | async-start | bytes 229376 | tf_op jit(solution)/shard_map/all_to_all | solution.py:132
Sparse Core Ops, SparseCore 0:
  69.3 31.8 all-reduce.2
where the time goes:
time: 112 us
  waiting for transfers between devices  31.8 us (28%)
  starting transfers between devices  21.6 us (19%)
  local copies, waits for them, and re-layouts  18.5 us (17%)
  between operations  14.4 us (13%)
  matrix products  10.8 us (10%)
  blocking collectives  10.3 us (9%)
  other arithmetic  4.32 us (4%)
    psum x1, waiting for transfers between devices, shards(): lax.psum(word_part.astype(jnp.bfloat16), 'rel').astype(jnp.float32)  11.7 us
    all_to_all x1, blocking collectives, shards(): lax.all_to_all(outgoing.astype(jnp.bfloat16), 'blk', split_axis=0, concat...  10.3 us
    unnamed x23, local copies, waits for them, and re-layouts  7.83 us
    all_to_all x1, waiting for transfers between devices, shards(): lax.all_to_all(picked, 'blk', split_axis=0, concat_axis=0, tiled=True)  7.65 us
    all_to_all x1, starting transfers between devices, shards(): lax.all_to_all(wanted, 'blk', split_axis=0, concat_axis=0, tiled=True)  7.39 us
    all_to_all x1, waiting for transfers between devices, shards(): lax.all_to_all(lax.all_to_all(outgoing.astype(jnp.bfloat16), 'blk', split...  4.26 us
    all_to_all x1, starting transfers between devices, shards(): lax.all_to_all(picked, 'blk', split_axis=0, concat_axis=0, tiled=True)  3.87 us
    all_to_all x1, waiting for transfers between devices, shards(): lax.all_to_all(lax.all_to_all(wanted, 'blk', split_axis=0, concat_axis=0,...  3.75 us
  transfers between devices with their start and end apart: 7, of which 6 were waited for; matrix products, arithmetic and copies ran while one was open for 13% of the time, Pallas kernels for 0%

commit v1 on v0

--- a/solution.py
+++ b/solution.py
@@ -124,8 +124,11 @@
         conj_product(query_grads, word_used.astype(jnp.float32), half_width),
     )
     slot_grad = slot_grad + 0.02 * live_mask[:, None] * slot_table.astype(jnp.float32)
+    show_the_sums_all = lambda field, axis_id: jnp.sum(
+        jax.lax.all_gather(field, axis_name=axis_id), axis=0
+    )
     word_sum, ctx_sum = (
-        lax.psum(word_part.astype(jnp.bfloat16), "rel").astype(jnp.float32),
+        show_the_sums_all(word_part.astype(jnp.bfloat16), "rel").astype(jnp.float32),
         lax.psum(ctx_part.astype(jnp.bfloat16), "rel").astype(jnp.float32),
     )
     outgoing = slot_grad.reshape(part_count, split_count, slot_count, row_width)

time: 112 us -> 117 us (1.045)
  waiting for transfers between devices: 31.8 us -> 21 us
  other arithmetic: 4.32 us -> 8.27 us
  starting transfers between devices: 21.6 us -> 25.5 us
  matrix products: 10.8 us -> 14.1 us
  blocking collectives: 10.3 us -> 13.4 us
    all_gather x0 -> x1, blocking collectives: none -> 13.4 us  [shards(): jax.lax.all_gather(field, axis_name=axis_id)]
    all_to_all x1 -> x0, blocking collectives: 10.3 us -> none  [shards(): lax.all_to_all(outgoing.astype(jnp.bfloat16), 'blk', split_axis=0, concat...]
    psum x1, waiting for transfers between devices: 11.7 us -> 2.63 us  [shards(): lax.psum(ctx_part.astype(jnp.bfloat16), 'rel').astype(jnp.float32)]
    all_to_all x1, waiting for transfers between devices: 4.26 us -> 0.01 us  [shards(): lax.all_to_all(lax.all_to_all(outgoing.astype(jnp.bfloat16), 'blk', split...]
    all_to_all x0 -> x1, starting transfers between devices: none -> 4.15 us  [shards(): lax.all_to_all(outgoing.astype(jnp.bfloat16), 'blk', split_axis=0, concat...]
    reduce_sum x0 -> x1, other arithmetic: none -> 2.93 us  [shards(): jnp.sum(jax.lax.all_gather(field, axis_name=axis_id), axis=0)]
    unnamed x23 -> x28, local copies, waits for them, and re-layouts: 7.83 us -> 5.7 us
    dot_general x4, matrix products: 2.33 us -> 4.39 us  [spread_rows(): jnp.dot(selector, upper, preferred_element_type=jnp.float32)]
  transfers between devices with their start and end apart: 7 -> 8, of which waited for: 6 -> 6; matrix products, arithmetic and copies ran while one was open for 13% -> 21% of each run, Pallas kernels for 0% -> 0%
where the time goes in v1:
time: 117 us; the launch traced here: 116 us
  starting transfers between devices  25.5 us (22%)
  waiting for transfers between devices  21 us (18%)
  local copies, waits for them, and re-layouts  19.1 us (16%)
  between operations  14.4 us (12%)
  matrix products  14.1 us (12%)
  blocking collectives  13.4 us (11%)
  other arithmetic  8.27 us (7%)
    all_gather x1, blocking collectives, shards(): jax.lax.all_gather(field, axis_name=axis_id)  13.4 us
    all_to_all x1, waiting for transfers between devices, shards(): lax.all_to_all(picked, 'blk', split_axis=0, concat_axis=0, tiled=True)  7.61 us
    all_to_all x1, starting transfers between devices, shards(): lax.all_to_all(wanted, 'blk', split_axis=0, concat_axis=0, tiled=True)  7.39 us
    unnamed x28, local copies, waits for them, and re-layouts  5.7 us
    dot_general x4, matrix products, spread_rows(): jnp.dot(selector, upper, preferred_element_type=jnp.float32)  4.39 us
    all_to_all x1, starting transfers between devices, shards(): lax.all_to_all(outgoing.astype(jnp.bfloat16), 'blk', split_axis=0, concat...  4.15 us
    all_to_all x1, waiting for transfers between devices, shards(): lax.all_to_all(lax.all_to_all(wanted, 'blk', split_axis=0, concat_axis=0,...  3.75 us
    dot_general x4, matrix products, spread_rows(): jnp.dot(selector, lower, preferred_element_type=jnp.float32)  3.57 us
  transfers between devices with their start and end apart: 8, of which 6 were waited for; matrix products, arithmetic and copies ran while one was open for 21% of the time, Pallas kernels for 0%

profile of v1, /device:TPU:0, one launch (start us, length us, event | category | flops | bytes accessed | tf_op | source)
XLA Modules:
  0.0 115.7 jit_solution(17299743178935162796)
XLA Ops:
  7.2 1.4 %copy.51 = s32[16,2,2]{2,1,0:T(2,128)} copy(s32[16,2,2]{0,2,1:T(2,128)} %bitcast.16) | data formatting | bytes 512 | tf_op jit(solution)/shard_map/squeeze | solution.py:54
  8.6 7.4 %all-to-all-start = ((s32[16,2,2]{2,1,0:T(2,128)}), s32[16,2,2]{2,1,0:T(2,128)S(1)}, u32[]{:S(2)}, u32[]{:S(2)}) async-start(s32[16,2,2]{2,1,0:T(2,128)} %copy.51), calls=%async_computation | async-start | bytes 32768 | tf_op jit(solution)/shard_map/all_to_all | solution.py:56
  16.0 1.2 %copy.57 = bf16[256,800]{1,0:T(8,128)(2,1)S(1)} copy(bf16[256,800]{0,1:T(8,128)(2,1)} %param.10) | data formatting | bytes 819200 | tf_op args[1]
  17.3 0.5 collective-permute-start
  17.7 0.7 compare_select_fusion.2
  18.4 0.7 compare_select_fusion.3
  19.1 0.8 copy.60
  19.8 0.1 compare_select_fusion
  19.9 2.6 %all-to-all-done = s32[16,2,2]{2,1,0:T(2,128)S(1)} async-done(((s32[16,2,2]{2,1,0:T(2,128)}), s32[16,2,2]{2,1,0:T(2,128)S(1)}, u32[]{:S(2)}, u32[]{:S(2)}) %all-to-all-start) | async-done | bytes 288 | tf_op jit(solution)/shard_map/all_to_all | solution.py:56
  22.5 0.7 copy.52
  23.2 3.2 %all-to-all-start.1 = ((s32[16,2,2]{0,2,1:T(2,128)}), s32[16,2,2]{0,2,1:T(2,128)S(1)}, u32[]{:S(2)}, u32[]{:S(2)}) async-start(s32[16,2,2]{0,2,1:T(2,128)} %copy.52), calls=%async_computation.1 | async-start | bytes 4096 | tf_op jit(solution)/shard_map/all_to_all | solution.py:55
  26.4 3.7 %all-to-all-done.1 = s32[16,2,2]{0,2,1:T(2,128)S(1)} async-done(((s32[16,2,2]{0,2,1:T(2,128)}), s32[16,2,2]{0,2,1:T(2,128)S(1)}, u32[]{:S(2)}, u32[]{:S(2)}) %all-to-all-start.1) | async-done | bytes 288 | tf_op jit(solution)/shard_map/all_to_all | solution.py:55
  30.2 0.1 copy.53
  30.3 0.1 reshape.85
  30.4 0.7 gather_fusion.1
  31.1 0.7 reshape.86
  31.8 3.5 %all-to-all-start.2 = ((bf16[16,2,2,800]{3,2,1,0:T(2,128)(2,1)}), bf16[16,2,2,800]{3,2,1,0:T(2,128)(2,1)S(1)}, u32[]{:S(2)}, u32[]{:S(2)}) async-start(bf16[16,2,2,800]{3,2,1,0:T(2,128)(2,1)} %reshape.86), calls=%async_computation.2 | async-start | bytes 229376 | tf_op jit(solution)/shard_map/all_to_all | solution.py:64
  35.4 7.6 %all-to-all-done.2 = bf16[16,2,2,800]{3,2,1,0:T(2,128)(2,1)S(1)} async-done(((bf16[16,2,2,800]{3,2,1,0:T(2,128)(2,1)}), bf16[16,2,2,800]{3,2,1,0:T(2,128)(2,1)S(1)}, u32[]{:S(2)}, u32[]{:S(2)}) %all-to-all-start.2) | async-done | bytes 102432 | tf_op jit(solution)/shard_map/all_to_all | solution.py:64
  43.0 0.7 copy.54
  43.7 3.4 %all-to-all-start.3 = ((bf16[16,2,2,800]{3,2,0,1:T(2,128)(2,1)}), bf16[16,2,2,800]{3,2,0,1:T(2,128)(2,1)S(1)}, u32[]{:S(2)}, u32[]{:S(2)}) async-start(bf16[16,2,2,800]{3,2,0,1:T(2,128)(2,1)} %copy.54), calls=%async_computation.3 | async-start | bytes 229376 | tf_op jit(solution)/shard_map/all_to_all | solution.py:63
  47.1 0.2 copy.49
  47.3 1.2 %gather_fusion = bf16[256,800]{1,0:T(8,128)(2,1)S(1)} fusion(bf16[256,800]{1,0:T(8,128)(2,1)S(1)} %copy.49, s32[1024]{0:T(1024)S(1)} %pad_clamp_fusion.3), kind=kCustom, calls=%fused_computation | custom fusion | bytes 820224 | tf_op jit(solution)/shard_map/gather | solution.py:77
  48.5 0.2 copy.50
  48.7 0.1 convert_element_type.93
  48.8 0.1 mul.94
  48.9 0.1 eq.86
  49.0 2.4 %all-to-all-done.3 = bf16[16,2,2,800]{3,2,0,1:T(2,128)(2,1)S(1)} async-done(((bf16[16,2,2,800]{3,2,0,1:T(2,128)(2,1)}), bf16[16,2,2,800]{3,2,0,1:T(2,128)(2,1)S(1)}, u32[]{:S(2)}, u32[]{:S(2)}) %all-to-all-start.3) | async-done | bytes 102432 | tf_op jit(solution)/shard_map/all_to_all | solution.py:63
  51.4 0.1 copy.55
  51.5 0.1 reshape.87
  51.6 1.2 %gather_fusion.2 = bf16[256,800]{1,0:T(8,128)(2,1)S(1)} fusion(bf16[64,800]{1,0:T(8,128)(2,1)S(1)} %reshape.87, s32[1024]{0:T(1024)S(1)} %pad_clamp_fusion.1), kind=kCustom, calls=%fused_computation.2 | custom fusion | bytes 820224 | tf_op jit(solution)/shard_map/gather | solution.py:79
  52.8 0.2 copy.56
  53.1 0.1 subtract_convert_fusion.8
  53.3 1.0 fusion.41
  54.3 2.4 %copy.66 = f32[256,800]{1,0:T(8,128)} copy(f32[256,800]{0,1:T(8,128)} %fusion.41) | data formatting | bytes 1638400
  56.7 0.7 convolution_convert_fusion
  57.3 0.9 fusion.6
  58.2 1.5 %fusion.42 = f32[256,800]{0,1:T(8,128)} fusion(bf16[256,1024]{1,0:T(8,128)(2,1)S(1)} %fusion.6, bf16[1024,800]{0,1:T(8,128)(2,1)S(1)} %convolution_convert_fusion), kind=kOutput, calls=%fused_computation.81 | convolution fusion | flops 419430400 | bytes 2981888 | tf_op jit(solution)/shard_map/while/body/eval_jaxpr/dot_general | solution.py:99
  59.7 2.3 %fusion.40 = f32[1024,800]{0,1:T(8,128)} fusion(bf16[256,1024]{1,0:T(8,128)(2,1)S(1)} %fusion.6, bf16[256,400]{0,1:T(8,128)(2,1)S(1)} %get-tuple-element.32, bf16[256,400]{0,1:T(8,128)(2,1)S(1)} %get-tuple-element.23), kind=kOutput, calls=%fused_computation.79 | convolution fusion | flops 420249600 | bytes 4210688 | tf_op jit(solution)/shard_map/while/body/eval_jaxpr/dot_general | solution.py:102
  62.0 1.2 %gather_fusion.3 = bf16[256,800]{1,0:T(8,128)(2,1)S(1)} fusion(bf16[256,800]{1,0:T(8,128)(2,1)S(1)} %collective-permute-done, s32[1024]{0:T(1024)S(1)} %pad_clamp_fusion), kind=kCustom, calls=%fused_computation.3 | custom fusion | bytes 820224 | tf_op jit(solution)/shard_map/gather | solution.py:78
  63.2 0.2 copy.58
  63.4 1.4 %multiply_reduce_fusion = f32[256]{0:T(256)S(1)} fusion(f32[256,800]{1,0:T(8,128)} %copy.66, bf16[256,800]{1,0:T(8,128)(2,1)S(1)} %gather_fusion.3), kind=kLoop, calls=%fused_computation.23 | loop fusion | flops 614144 | bytes 1229824 | tf_op jit(solution)/shard_map/td,td->t/dot_general | solution.py:83
  64.9 1.2 %fusion.15 = f32[256,800]{0,1:T(8,128)} fusion(f32[256]{0:T(256)S(1)} %divide_negate_fusion, s32[256]{0:T(256)S(1)} %copy-done.10, bf16[256,400]{0,1:T(8,128)(2,1)S(1)} %get-tuple-element.32, bf16[256,400]{0,1:T(8,128)(2,1)S(1)} %get-tuple-element.23), kind=kOutput, calls=%fused_computation.35 | convolution fusion | flops 106151936 | bytes 1230848 | tf_op jit(solution)/shard_map/dot_general | solution.py:35
  66.1 0.1 multiply_add_fusion
  66.2 1.1 multiply_add_fusion.1
  67.2 0.3 fusion.21
  67.5 0.9 fusion.10
  68.5 1.7 %convert_element_type.115 = bf16[16,2,2,800]{3,2,1,0:T(2,128)(2,1)} reshape(bf16[64,800]{1,0:T(8,128)(2,1)} %fusion.10) | data formatting | bytes 204800 | tf_op jit(solution)/shard_map/convert_element_type | solution.py:137
  70.1 4.1 %all-to-all-start.4 = ((bf16[16,2,2,800]{3,2,1,0:T(2,128)(2,1)}), bf16[16,2,2,800]{3,2,1,0:T(2,128)(2,1)}, u32[]{:S(2)}, u32[]{:S(2)}) async-start(bf16[16,2,2,800]{3,2,1,0:T(2,128)(2,1)} %convert_element_type.115), calls=%async_computation.4 | async-start | bytes 229376 | tf_op jit(solution)/shard_map/all_to_all | solution.py:136
  74.4 1.7 %convolution_add_fusion.1 = f32[256,800]{0,1:T(8,128)S(1)} fusion(f32[256,800]{0,1:T(8,128)} %fusion.15, f32[256]{0:T(256)S(1)} %divide_negate_fusion, s32[256]{0:T(256)S(1)} %copy-done.10, bf16[256,400]{0,1:T(8,128)(2,1)} %copy-done.3, bf16[256,400]{0,1:T(8,128)(2,1)} %copy-done.2), kind=kOutput, calls=%fused_computation.14 | convolution fusion | flops 106971136 | bytes 2050048 | tf_op jit(solution)/shard_map/dot_general | solution.py:35
  76.1 0.7 fusion
  76.7 1.4 %fusion.8 = bf16[256,800]{0,1:T(8,128)(2,1)} fusion(f32[256,800]{0,1:T(8,128)S(1)} %convolution_add_fusion.1, f32[256,800]{0,1:T(8,128)S(1)} %fusion, f32[1024,800]{0,1:T(8,128)S(1)} %copy-done.1, s32[1024]{0:T(1024)S(1)} %bitcast.15), kind=kOutput, calls=%fused_computation.18 | convolution fusion | flops 421126144 | bytes 5328896 | tf_op jit(solution)/shard_map/while/body/eval_jaxpr/dot_general | solution.py:35
  78.2 1.5 %fusion.19 = f32[256,800]{0,1:T(8,128)S(1)} fusion(f32[256,400]{0,1:T(8,128)} %get-tuple-element.33, f32[256,400]{0,1:T(8,128)} %get-tuple-element.34, s32[256]{0:T(256)S(1)} %copy-done.9), kind=kOutput, calls=%fused_computation.39 | convolution fusion | flops 105742336 | bytes 1639424 | tf_op jit(solution)/shard_map/dot_general | solution.py:35
  79.7 0.3 fusion.7
  80.0 2.0 %all-to-all-done.4 = bf16[16,2,2,800]{3,2,1,0:T(2,128)(2,1)} async-done(((bf16[16,2,2,800]{3,2,1,0:T(2,128)(2,1)}), bf16[16,2,2,800]{3,2,1,0:T(2,128)(2,1)}, u32[]{:S(2)}, u32[]{:S(2)}) %all-to-all-start.4) | async-done | bytes 102432 | tf_op jit(solution)/shard_map/all_to_all | solution.py:136
  82.0 1.6 %copy.61 = bf16[16,2,2,800]{3,2,0,1:T(2,128)(2,1)} copy(bf16[16,2,2,800]{3,2,1,0:T(2,128)(2,1)} %all-to-all-done.4) | data formatting | bytes 204800 | tf_op jit(solution)/shard_map/all_to_all | solution.py:136
  83.6 3.4 %all-to-all-start.5 = ((bf16[16,2,2,800]{3,2,0,1:T(2,128)(2,1)}), bf16[16,2,2,800]{3,2,0,1:T(2,128)(2,1)S(1)}, u32[]{:S(2)}, u32[]{:S(2)}) async-start(bf16[16,2,2,800]{3,2,0,1:T(2,128)(2,1)} %copy.61), calls=%async_computation.5 | async-start | bytes 229376 | tf_op jit(solution)/shard_map/all_to_all | solution.py:135
  87.0 13.4 %all-gather = bf16[512,800]{0,1:T(8,128)(2,1)S(1)} all-gather(bf16[256,800]{0,1:T(8,128)(2,1)S(1)} %fusion.7), channel_id=2, replica_groups=mesh['blk'=16,'rel'=2] {'rel'}, dimensions={0}, use_global_device_ids=true | all-gather | bytes 1228800 | tf_op jit(solution)/shard_map/all_gather | solution.py:128
  100.4 0.2 reshape.121
  100.6 2.9 %reduce_sum.12 = bf16[256,800]{0,1:T(8,128)(2,1)} reduce(bf16[2,256,800]{1,0,2:T(2,128)(2,1)S(1)} %reshape.121, bf16[]{:T(256)} %constant.24.clone.1), dimensions={0}, to_apply=%region_0.1 | reduce | flops 204800 | bytes 1228802 | tf_op jit(solution)/shard_map/reduce_sum | solution.py:127
  103.5 0.1 copy.62
  103.6 0.1 reshape.88
  103.7 0.8 fusion.33
  104.5 2.6 %all-reduce.2.cloned.1.call-done = bf16[256,800]{0,1:T(8,128)(2,1)} async-done(((bf16[256,800]{0,1:T(8,128)(2,1)}), bf16[256,800]{0,1:T(8,128)(2,1)}) %all-reduce.2.cloned.1.call-update) | async-done | bytes 409616 | tf_op jit(solution)/shard_map/psum | solution.py:132
  107.1 1.8 %copy.68 = bf16[256,800]{0,1:T(8,128)(2,1)} copy(bf16[256,800]{0,1:T(8,128)(2,1)} %all-reduce.2.cloned.1.call-done) | data formatting | bytes 819200
  (36 shorter events, 0.2 us)
Async XLA Ops:
  7.2 23.2 %copy-start = (bf16[32,800]{1,0:T(8,128)(2,1)S(1)}, bf16[32,800]{1,0:T(8,128)(2,1)}, u32[]{:S(2)}) copy-start(bf16[32,800]{1,0:T(8,128)(2,1)} %param.11) | copy-start | bytes 153604
  7.2 28.2 %copy-start.10 = (s32[256]{0:T(256)S(1)}, s32[256]{0:T(256)}, u32[]{:S(2)}) copy-start(s32[256]{0:T(256)} %param.13) | copy-start | bytes 3076
  7.2 39.9 %copy-start.7 = (bf16[256,800]{0,1:T(8,128)(2,1)S(1)}, bf16[256,800]{0,1:T(8,128)(2,1)}, u32[]{:S(2)}) copy-start(bf16[256,800]{0,1:T(8,128)(2,1)} %param.9) | copy-start | bytes 1228804
  8.6 13.9 %all-to-all-start = ((s32[16,2,2]{2,1,0:T(2,128)}), s32[16,2,2]{2,1,0:T(2,128)S(1)}, u32[]{:S(2)}, u32[]{:S(2)}) async-start(s32[16,2,2]{2,1,0:T(2,128)} %copy.51), calls=%async_computation | async-start | bytes 32768 | tf_op jit(solution)/shard_map/all_to_all | solution.py:56
  17.3 39.4 %collective-permute-start = (bf16[256,800]{1,0:T(8,128)(2,1)S(1)}, bf16[256,800]{1,0:T(8,128)(2,1)S(1)}, u32[]{:S(2)}, u32[]{:S(2)}) collective-permute-start(bf16[256,800]{1,0:T(8,128)(2,1)S(1)} %copy.57), channel_id=1, source_target_pairs={{0,2},{2,4},{4,6},{6,8},{8,10},{10,12},{12,14},{14,16},{16,18},{18... | collective-permute-start | bytes 1228808 | tf_op jit(solution)/shard_map/ppermute | solution.py:9
  23.2 7.0 %all-to-all-start.1 = ((s32[16,2,2]{0,2,1:T(2,128)}), s32[16,2,2]{0,2,1:T(2,128)S(1)}, u32[]{:S(2)}, u32[]{:S(2)}) async-start(s32[16,2,2]{0,2,1:T(2,128)} %copy.52), calls=%async_computation.1 | async-start | bytes 4096 | tf_op jit(solution)/shard_map/all_to_all | solution.py:55
  31.8 11.2 %all-to-all-start.2 = ((bf16[16,2,2,800]{3,2,1,0:T(2,128)(2,1)}), bf16[16,2,2,800]{3,2,1,0:T(2,128)(2,1)S(1)}, u32[]{:S(2)}, u32[]{:S(2)}) async-start(bf16[16,2,2,800]{3,2,1,0:T(2,128)(2,1)} %reshape.86), calls=%async_computation.2 | async-start | bytes 229376 | tf_op jit(solution)/shard_map/all_to_all | solution.py:64
  43.7 7.7 %all-to-all-start.3 = ((bf16[16,2,2,800]{3,2,0,1:T(2,128)(2,1)}), bf16[16,2,2,800]{3,2,0,1:T(2,128)(2,1)S(1)}, u32[]{:S(2)}, u32[]{:S(2)}) async-start(bf16[16,2,2,800]{3,2,0,1:T(2,128)(2,1)} %copy.54), calls=%async_computation.3 | async-start | bytes 229376 | tf_op jit(solution)/shard_map/all_to_all | solution.py:63
  53.2 11.6 %copy-start.2 = (bf16[256,400]{0,1:T(8,128)(2,1)}, bf16[256,400]{0,1:T(8,128)(2,1)S(1)}, u32[]{:S(2)}) copy-start(bf16[256,400]{0,1:T(8,128)(2,1)S(1)} %get-tuple-element.23) | copy-start | bytes 614404
  53.2 11.6 %copy-start.3 = (bf16[256,400]{0,1:T(8,128)(2,1)}, bf16[256,400]{0,1:T(8,128)(2,1)S(1)}, u32[]{:S(2)}) copy-start(bf16[256,400]{0,1:T(8,128)(2,1)S(1)} %get-tuple-element.32) | copy-start | bytes 614404
  53.2 3.4 %copy-start.8 = (s32[1,1024]{1,0:T(1,128)S(1)}, s32[1,1024]{1,0:T(1,128)}, u32[]{:S(2)}) copy-start(s32[1,1024]{1,0:T(1,128)} %param.15) | copy-start | bytes 12292
  63.4 2.7 %copy-start.6 = (f32[256,800]{0,1:T(8,128)S(1)}, f32[256,800]{0,1:T(8,128)}, u32[]{:S(2)}) copy-start(f32[256,800]{0,1:T(8,128)} %fusion.42) | copy-start | bytes 2457604
  66.2 1.1 copy-start.11
  67.5 8.5 %copy-start.1 = (f32[1024,800]{0,1:T(8,128)S(1)}, f32[1024,800]{0,1:T(8,128)}, u32[]{:S(2)}) copy-start(f32[1024,800]{0,1:T(8,128)} %fusion.40) | copy-start | bytes 9830404
  70.1 11.8 %all-to-all-start.4 = ((bf16[16,2,2,800]{3,2,1,0:T(2,128)(2,1)}), bf16[16,2,2,800]{3,2,1,0:T(2,128)(2,1)}, u32[]{:S(2)}, u32[]{:S(2)}) async-start(bf16[16,2,2,800]{3,2,1,0:T(2,128)(2,1)} %convert_element_type.115), calls=%async_computation.4 | async-start | bytes 229376 | tf_op jit(solution)/shard_map/all_to_all | solution.py:136
  74.3 32.8 %all-reduce.2.cloned.1.call-start = ((), (), s32[]{:S(2)}) async-start(), calls=%async_computation.6 | async-start | bytes 819200 | tf_op jit(solution)/shard_map/psum | solution.py:132
  76.7 1.5 %copy-start.9 = (s32[256]{0:T(256)S(1)}, s32[256]{0:T(256)}, u32[]{:S(2)}) copy-start(s32[256]{0:T(256)} %param.12) | copy-start | bytes 3076
  78.1 1.5 %copy-start.4 = (f32[256,400]{0,1:T(8,128)S(1)}, f32[256,400]{0,1:T(8,128)}, u32[]{:S(2)}) copy-start(f32[256,400]{0,1:T(8,128)} %get-tuple-element.33) | copy-start | bytes 1228804
  78.1 1.5 %copy-start.5 = (f32[256,400]{0,1:T(8,128)S(1)}, f32[256,400]{0,1:T(8,128)}, u32[]{:S(2)}) copy-start(f32[256,400]{0,1:T(8,128)} %get-tuple-element.34) | copy-start | bytes 1228804
  83.6 19.9 %all-to-all-start.5 = ((bf16[16,2,2,800]{3,2,0,1:T(2,128)(2,1)}), bf16[16,2,2,800]{3,2,0,1:T(2,128)(2,1)S(1)}, u32[]{:S(2)}, u32[]{:S(2)}) async-start(bf16[16,2,2,800]{3,2,0,1:T(2,128)(2,1)} %copy.61), calls=%async_computation.5 | async-start | bytes 229376 | tf_op jit(solution)/shard_map/all_to_all | solution.py:135
Sparse Core Ops, SparseCore 0:
  78.3 28.7 all-reduce.1
